TPU v7x, 256 devices: a whole 4x4x8 slice. The times are simulated.
256 devices in a mesh: row: 32 (over z, y_hi, core), col: 8 (over x, y_lo).
Axes of the slice: x: 4, y: 4 (y_hi: 2, y_lo: 2; y = y_hi * 2 + y_lo), z: 8, core: 2. Of those that a mesh axis runs over, the one named last changes fastest.
Arguments:
- affinity_tiles: bfloat16 [1024, 512, 512], P(('row', 'col')), may hold values from -6 to 6
- tile_rows: int32 [1024], P(('row', 'col')), may hold values from -1 to 63, as said below
- tile_cols: int32 [1024], P(('row', 'col')), may hold values from -1 to 63, as said below
- lang_counts: int32 [32], replicated, may hold values from 1 to 8192, 32768 in all
- start_basis: float32 [8, 4096, 64], P('col', 'row'), may hold values from -6 to 6
Outputs:
- eigen_basis: float32 [8, 4096, 64], P('col', 'row')
Inputs may be any that keep to these rules, and one draw needn't show every extreme that they name: `tile_rows`: the slots of device (r, c) are entries (r * 8 + c) * 4 onward of both lists. Every used slot names a distinct block with block row from r * 2 to (r + 1) * 2 - 1, block column from c * 8 to (c + 1) * 8 - 1, and block row <= block column; no block is named twice. Empty slots hold -1 in both lists and come after the used slots of their device. Device (0, 7) uses all 4 slots. `tile_cols`: same slots as tile_rows.
All inputs are finite; a program needn't handle non-finite values.
Results may differ from a plain program's by a relative error of at most 0.0044.
Values may be sent and summed in bfloat16 or wider, within the bound.
No kernel may reach another device: no remote copies, remote signals or barrier semaphores. Data moves between devices by JAX's collectives and lax.ppermute only.
A program may use at most 64 MiB of HBM per device.

v0:
```python
import jax
import jax.numpy as jnp
from jax import lax
from jax.sharding import PartitionSpec as P

ROW_BLOCKS = 2
ITERS = 3
highest = lax.Precision.HIGHEST


def broadcast(value, axis, root):
    mine = lax.axis_index(axis) == root
    return lax.psum(jnp.where(mine, value, jnp.zeros_like(value)), axis)


def add_block(target, addend, offset):
    current = lax.dynamic_slice_in_dim(target, offset, addend.shape[0], 0)
    return lax.dynamic_update_slice_in_dim(target, current + addend, offset, 0)


def membership(first_doc, doc_count, lang_ends, lang_starts):
    doc_index = first_doc + jnp.arange(doc_count, dtype=jnp.int32)
    return (
        (doc_index[:, None] >= lang_starts[None, :]) & (doc_index[:, None] < lang_ends[None, :])
    ).astype(jnp.float32)


def apply_tiles(affinity_tiles, pick_rows, pick_cols, scaled_rows, scaled_cols, col_blocks):
    slot_count, tile_size, _ = affinity_tiles.shape
    vectors = scaled_cols.shape[1]
    blocks_r = scaled_rows.reshape(ROW_BLOCKS, tile_size, vectors)
    blocks_c = scaled_cols.reshape(col_blocks, tile_size, vectors)
    chosen_c = jnp.einsum(
        "tq,qjk->tjk", pick_cols, blocks_c, preferred_element_type=jnp.float32
    ).astype(jnp.bfloat16)
    chosen_r = jnp.einsum(
        "tp,pik->tik", pick_rows, blocks_r, preferred_element_type=jnp.float32
    ).astype(jnp.bfloat16)
    forward = jnp.einsum(
        "tij,tjk->tik", affinity_tiles, chosen_c, preferred_element_type=jnp.float32
    )
    backward = jnp.einsum(
        "tij,tik->tjk", affinity_tiles, chosen_r, preferred_element_type=jnp.float32
    )
    part_rows = jnp.einsum("tp,tik->pik", pick_rows.astype(jnp.float32), forward, precision=highest)
    part_cols = jnp.einsum(
        "tq,tjk->qjk", pick_cols.astype(jnp.float32), backward, precision=highest
    )
    return (
        part_rows.reshape(ROW_BLOCKS * tile_size, vectors),
        part_cols.reshape(col_blocks * tile_size, vectors),
    )


def shards(affinity_tiles, tile_rows, tile_cols, lang_counts, start_basis):
    row_devices = lax.axis_size("row")
    col_devices = lax.axis_size("col")
    group_ratio = row_devices // col_devices
    col_blocks = ROW_BLOCKS * row_devices // col_devices
    tile_size = affinity_tiles.shape[1]
    row_span = ROW_BLOCKS * tile_size
    col_span = col_blocks * tile_size
    piece_rows = start_basis.shape[1]
    doc_total = piece_rows * row_devices * col_devices
    my_row = lax.axis_index("row")
    my_col = lax.axis_index("col")
    is_owner = (my_row // group_ratio == my_col).astype(jnp.float32)
    offset = my_row % group_ratio * row_span
    piece_offset = my_row * piece_rows
    present = tile_rows >= 0
    local_p = tile_rows - my_row * ROW_BLOCKS
    local_q = tile_cols - my_col * col_blocks
    pick_rows = (
        (local_p[:, None] == jnp.arange(ROW_BLOCKS, dtype=jnp.int32)[None, :]) & present[:, None]
    ).astype(jnp.bfloat16)
    pick_cols = (
        (local_q[:, None] == jnp.arange(col_blocks, dtype=jnp.int32)[None, :]) & present[:, None]
    ).astype(jnp.bfloat16)
    magnitude = jnp.abs(affinity_tiles)
    row_mass = jnp.sum(magnitude, axis=2, dtype=jnp.float32)
    col_mass = jnp.sum(magnitude, axis=1, dtype=jnp.float32)
    degree_rows = jnp.einsum(
        "tp,ti->pi", pick_rows.astype(jnp.float32), row_mass, precision=highest
    ).reshape(row_span)
    degree_cols = jnp.einsum(
        "tq,tj->qj", pick_cols.astype(jnp.float32), col_mass, precision=highest
    ).reshape(col_span)
    rows_degree = lax.psum(degree_rows, "col")
    degree_cols = add_block(degree_cols, is_owner * rows_degree, offset)
    inv_own = lax.rsqrt(1.0 + lax.psum_scatter(degree_cols, "row", scatter_dimension=0, tiled=True))
    prior_scale = lax.psum(jnp.sum(inv_own), ("row", "col")) / doc_total
    lang_ends = jnp.cumsum(lang_counts)
    lang_starts = lang_ends - lang_counts
    counts_real = lang_counts.astype(jnp.float32)
    member_own = membership(my_col * col_span + piece_offset, piece_rows, lang_ends, lang_starts)
    basis_own = start_basis[0]
    for iteration in range(ITERS):
        lang_now = lax.psum(jnp.dot(member_own.T, basis_own, precision=highest), ("row", "col"))
        lang_mean = prior_scale * (lang_now / counts_real[:, None])
        scaled_cols = lax.all_gather(
            (inv_own[:, None] * basis_own).astype(jnp.bfloat16), "row", axis=0, tiled=True
        )
        scaled_rows = broadcast(
            lax.dynamic_slice_in_dim(scaled_cols, offset, row_span, 0), "col", my_row // group_ratio
        )
        part_rows, part_cols = apply_tiles(
            affinity_tiles, pick_rows, pick_cols, scaled_rows, scaled_cols, col_blocks
        )
        rows_sum = lax.psum(part_rows, "col")
        part_cols = add_block(part_cols, is_owner * rows_sum, offset)
        product_own = lax.psum_scatter(part_cols, "row", scatter_dimension=0, tiled=True)
        applied_own = inv_own[:, None] * product_own + jnp.dot(
            member_own, lang_mean, precision=highest
        )
        gram_part = jnp.dot(applied_own.T, applied_own, precision=highest)
        gram_matrix = lax.psum(gram_part, ("row", "col"))
        factor = jnp.linalg.cholesky(gram_matrix / doc_total)
        basis_own = jax.scipy.linalg.solve_triangular(factor, applied_own.T, lower=True).T
    return basis_own[None]


def solution(mesh):
    in_specs = (
        P(("row", "col"), None, None),
        P(("row", "col")),
        P(("row", "col")),
        P(),
        P("col", "row", None),
    )
    out_specs = P("col", "row", None)
    return jax.shard_map(shards, mesh=mesh, in_specs=in_specs, out_specs=out_specs, check_vma=False)
```

profile of v0, /device:TPU:1, one launch (start us, length us, event | category | flops | bytes accessed | tf_op | source)
XLA Modules:
  0.0 1385.8 jit_solution(9308302912916534671)
XLA Ops:
  8.6 2.2 convert_reduce_fusion
  11.0 16.9 %psum.98 = f32[1024]{0:T(1024)S(1)} all-reduce(f32[1024]{0:T(1024)S(1)} %bitcast.181), channel_id=1, replica_groups=mesh['row'=32,'col'=8] {'col'}, use_global_device_ids=true, to_apply=%region_2.3 | all-reduce | flops 1024 | bytes 8192 | tf_op jit(solution)/shard_map/psum | solution.py:88
  28.1 130.8 %all-reduce = f32[4096]{0:T(1024)S(1)} all-reduce(f32[4096]{0:T(1024)S(1)} %add_dynamic-update-slice_fusion.3), channel_id=2, replica_groups=mesh['row'=32,'col'=8] {'row'}, use_global_device_ids=true, to_apply=%region_3.4.clone | all-reduce | flops 4096 | bytes 32768
  160.8 43.6 %all_gather.9 = bf16[4096,64]{0,1:T(8,128)(2,1)S(1)} all-gather(bf16[128,64]{0,1:T(8,128)(2,1)S(1)} %fusion.39), channel_id=1, replica_groups=mesh['row'=32,'col'=8] {'row'}, dimensions={0}, use_global_device_ids=true | all-gather | bytes 540672 | tf_op jit(solution)/shard_map/all_gather | solution.py:100
  206.5 0.9 fusion.8
  207.4 0.7 copy.46
  208.2 67.3 %all-reduce.9.cloned.1.call-done = bf16[2,512,64]{1,0,2:T(2,128)(2,1)} async-done(((bf16[2,512,64]{1,0,2:T(2,128)(2,1)}), bf16[2,512,64]{1,0,2:T(2,128)(2,1)}) %all-reduce.9.cloned.1.call-update) | async-done | bytes 131088 | tf_op jit(solution)/shard_map/psum | solution.py:13
  275.5 1.2 convolution_convert_fusion.5
  277.2 1.0 fusion.10
  278.9 77.9 %all-reduce.11.cloned.1.call-done = f32[1024,64]{0,1:T(8,128)} async-done(((f32[1024,64]{0,1:T(8,128)}), f32[1024,64]{0,1:T(8,128)}) %all-reduce.11.cloned.1.call-update) | async-done | bytes 262160 | tf_op jit(solution)/shard_map/psum | solution.py:109
  356.7 1.0 add_dynamic-update-slice_fusion.2
  357.7 1.0 copy-done.2
  359.3 79.9 %all-reduce.1 = (f32[32,64]{1,0:T(8,128)S(1)}, f32[]{:T(128)}) all-reduce(f32[32,64]{1,0:T(8,128)S(1)} %fusion.22, f32[]{:T(128)} %get-tuple-element.11), channel_id=1, replica_groups=mesh['row'=32,'col'=8] {'row','col'}, use_global_device_ids=true, to_apply=%region_10.11 | all-reduce | flops 2049 | bytes 16392 | tf_op jit(solution)/shard_map/psum | solution.py:98
  439.9 36.3 %reduce-scatter.4.cloned.1.call-done = f32[128,64]{0,1:T(8,128)} async-done(((f32[4096,64]{0,1:T(8,128)}), f32[128,64]{0,1:T(8,128)}) %reduce-scatter.4.cloned.1.call-update) | async-done | bytes 32784 | tf_op jit(solution)/shard_map/reduce_scatter | solution.py:111
  476.2 1.1 convolution_add_fusion.2
  477.4 79.7 %psum.103 = f32[64,64]{0,1:T(8,128)S(1)} all-reduce(f32[64,64]{0,1:T(8,128)S(1)} %fusion.75), channel_id=1, replica_groups=mesh['row'=32,'col'=8] {'row','col'}, use_global_device_ids=true, to_apply=%region_11.12 | all-reduce | flops 4096 | bytes 32768 | tf_op jit(solution)/shard_map/psum | solution.py:116
  557.2 5.8 cholesky.59
  564.4 4.9 custom-call.7
  569.6 41.2 %all_gather.10 = bf16[4096,64]{0,1:T(8,128)(2,1)S(1)} all-gather(bf16[128,64]{0,1:T(8,128)(2,1)S(1)} %fusion.44), channel_id=1, replica_groups=mesh['row'=32,'col'=8] {'row'}, dimensions={0}, use_global_device_ids=true | all-gather | bytes 540672 | tf_op jit(solution)/shard_map/all_gather | solution.py:100
  613.0 0.9 fusion.4
  613.9 0.7 copy.49
  614.7 65.5 %all-reduce.13.cloned.1.call-done = bf16[2,512,64]{1,0,2:T(2,128)(2,1)} async-done(((bf16[2,512,64]{1,0,2:T(2,128)(2,1)}), bf16[2,512,64]{1,0,2:T(2,128)(2,1)}) %all-reduce.13.cloned.1.call-update) | async-done | bytes 131088 | tf_op jit(solution)/shard_map/psum | solution.py:13
  680.2 1.2 convolution_convert_fusion.4
  681.9 1.0 fusion.6
  683.5 77.7 %all-reduce.15.cloned.1.call-done = f32[1024,64]{0,1:T(8,128)} async-done(((f32[1024,64]{0,1:T(8,128)}), f32[1024,64]{0,1:T(8,128)}) %all-reduce.15.cloned.1.call-update) | async-done | bytes 262160 | tf_op jit(solution)/shard_map/psum | solution.py:109
  761.2 1.0 add_dynamic-update-slice_fusion.1
  762.2 1.0 copy-done.3
  763.5 79.8 %psum.106 = f32[32,64]{1,0:T(8,128)S(1)} all-reduce(f32[32,64]{1,0:T(8,128)S(1)} %fusion.20), channel_id=1, replica_groups=mesh['row'=32,'col'=8] {'row','col'}, use_global_device_ids=true, to_apply=%region_17.20 | all-reduce | flops 2048 | bytes 16384 | tf_op jit(solution)/shard_map/psum | solution.py:98
  843.3 37.3 %reduce-scatter.6.cloned.1.call-done = f32[128,64]{0,1:T(8,128)} async-done(((f32[4096,64]{0,1:T(8,128)}), f32[128,64]{0,1:T(8,128)}) %reduce-scatter.6.cloned.1.call-update) | async-done | bytes 32784 | tf_op jit(solution)/shard_map/reduce_scatter | solution.py:111
  880.5 1.1 convolution_add_fusion.1
  881.8 79.7 %psum.107 = f32[64,64]{0,1:T(8,128)S(1)} all-reduce(f32[64,64]{0,1:T(8,128)S(1)} %fusion.76), channel_id=1, replica_groups=mesh['row'=32,'col'=8] {'row','col'}, use_global_device_ids=true, to_apply=%region_18.21 | all-reduce | flops 4096 | bytes 32768 | tf_op jit(solution)/shard_map/psum | solution.py:116
  961.6 5.8 cholesky.70
  968.8 4.9 custom-call.8
  974.0 41.2 %all_gather.11 = bf16[4096,64]{0,1:T(8,128)(2,1)S(1)} all-gather(bf16[128,64]{0,1:T(8,128)(2,1)S(1)} %fusion.45), channel_id=1, replica_groups=mesh['row'=32,'col'=8] {'row'}, dimensions={0}, use_global_device_ids=true | all-gather | bytes 540672 | tf_op jit(solution)/shard_map/all_gather | solution.py:100
  1017.2 0.9 fusion
  1019.1 65.4 %all-reduce.17.cloned.1.call-done = bf16[2,512,64]{1,0,2:T(2,128)(2,1)} async-done(((bf16[2,512,64]{1,0,2:T(2,128)(2,1)}), bf16[2,512,64]{1,0,2:T(2,128)(2,1)}) %all-reduce.17.cloned.1.call-update) | async-done | bytes 131088 | tf_op jit(solution)/shard_map/psum | solution.py:13
  1084.6 1.2 convolution_convert_fusion.3
  1086.3 1.0 fusion.2
  1087.9 77.9 %all-reduce.19.cloned.1.call-done = f32[1024,64]{0,1:T(8,128)} async-done(((f32[1024,64]{0,1:T(8,128)}), f32[1024,64]{0,1:T(8,128)}) %all-reduce.19.cloned.1.call-update) | async-done | bytes 262160 | tf_op jit(solution)/shard_map/psum | solution.py:109
  1165.7 1.0 add_dynamic-update-slice_fusion
  1166.8 1.0 copy-done.1
  1168.0 79.8 %psum.110 = f32[32,64]{1,0:T(8,128)S(1)} all-reduce(f32[32,64]{1,0:T(8,128)S(1)} %fusion.18), channel_id=1, replica_groups=mesh['row'=32,'col'=8] {'row','col'}, use_global_device_ids=true, to_apply=%region_22.25 | all-reduce | flops 2048 | bytes 16384 | tf_op jit(solution)/shard_map/psum | solution.py:98
  1247.8 37.4 %reduce-scatter.8.cloned.1.call-done = f32[128,64]{0,1:T(8,128)} async-done(((f32[4096,64]{0,1:T(8,128)}), f32[128,64]{0,1:T(8,128)}) %reduce-scatter.8.cloned.1.call-update) | async-done | bytes 32784 | tf_op jit(solution)/shard_map/reduce_scatter | solution.py:111
  1285.2 1.1 convolution_add_fusion
  1286.5 79.7 %psum.111 = f32[64,64]{0,1:T(8,128)S(1)} all-reduce(f32[64,64]{0,1:T(8,128)S(1)} %fusion.77), channel_id=1, replica_groups=mesh['row'=32,'col'=8] {'row','col'}, use_global_device_ids=true, to_apply=%region_23.26 | all-reduce | flops 4096 | bytes 32768 | tf_op jit(solution)/shard_map/psum | solution.py:116
  1366.3 5.8 cholesky.81
  1373.5 4.9 custom-call.9
  1378.4 0.9 convolution_bitcast_fusion.6
  (97 shorter events, 20.6 us)
Async XLA Ops:
  6.5 152.4 %copy-start.6 = (u32[256]{0:T(256)S(1)}, u32[256]{0:T(256)}, u32[]{:S(2)}) copy-start(u32[256]{0:T(256)} %constant.105) | copy-start | bytes 3076
  6.5 154.3 %copy-start.4 = (f32[1,128,64]{1,2,0:T(8,128)S(1)}, f32[1,128,64]{1,2,0:T(8,128)}, u32[]{:S(2)}) copy-start(f32[1,128,64]{1,2,0:T(8,128)} %param.12) | copy-start | bytes 98308
  6.5 269.0 %all-reduce.9.cloned.1.call-start = ((), (), s32[]{:S(2)}) async-start(), calls=%async_computation.3 | async-start | bytes 262144 | tf_op jit(solution)/shard_map/psum | solution.py:13
  10.8 194.9 %copy-start = (bf16[4,512,512]{2,1,0:T(8,128)(2,1)S(1)}, bf16[4,512,512]{2,1,0:T(8,128)(2,1)}, u32[]{:S(2)}) copy-start(bf16[4,512,512]{2,1,0:T(8,128)(2,1)} %param.8) | copy-start | bytes 6291460
  205.2 151.5 %all-reduce.11.cloned.1.call-start = ((), (), s32[]{:S(2)}) async-start(), calls=%async_computation.4 | async-start | bytes 524288 | tf_op jit(solution)/shard_map/psum | solution.py:109
  208.2 268.0 %reduce-scatter.4.cloned.1.call-start = ((), (), s32[]{:S(2)}) async-start(), calls=%async_computation.5 | async-start | bytes 1081344 | tf_op jit(solution)/shard_map/reduce_scatter | solution.py:111
  278.2 80.6 %copy-start.5 = (s32[32]{0:T(128)S(1)}, s32[32]{0:T(128)}, u32[]{:S(2)}) copy-start(s32[32]{0:T(128)} %param.11) | copy-start | bytes 388
  357.7 1.0 copy-start.2
  358.7 321.4 %all-reduce.13.cloned.1.call-start = ((), (), s32[]{:S(2)}) async-start(), calls=%async_computation.6 | async-start | bytes 262144 | tf_op jit(solution)/shard_map/psum | solution.py:13
  611.5 149.7 %all-reduce.15.cloned.1.call-start = ((), (), s32[]{:S(2)}) async-start(), calls=%async_computation.7 | async-start | bytes 524288 | tf_op jit(solution)/shard_map/psum | solution.py:109
  614.6 265.9 %reduce-scatter.6.cloned.1.call-start = ((), (), s32[]{:S(2)}) async-start(), calls=%async_computation.8 | async-start | bytes 1081344 | tf_op jit(solution)/shard_map/reduce_scatter | solution.py:111
  762.2 1.0 copy-start.3
  763.2 321.3 %all-reduce.17.cloned.1.call-start = ((), (), s32[]{:S(2)}) async-start(), calls=%async_computation.9 | async-start | bytes 262144 | tf_op jit(solution)/shard_map/psum | solution.py:13
  1015.9 149.9 %all-reduce.19.cloned.1.call-start = ((), (), s32[]{:S(2)}) async-start(), calls=%async_computation.10 | async-start | bytes 524288 | tf_op jit(solution)/shard_map/psum | solution.py:109
  1018.8 266.4 %reduce-scatter.8.cloned.1.call-start = ((), (), s32[]{:S(2)}) async-start(), calls=%async_computation.11 | async-start | bytes 1081344 | tf_op jit(solution)/shard_map/reduce_scatter | solution.py:111
  1166.8 1.0 copy-start.1
Sparse Core Ops, SparseCore 0:
  205.3 70.1 all-reduce.8
  278.1 78.5 all-reduce.10
  360.8 115.3 reduce-scatter.3
  611.6 68.4 all-reduce.12
  682.6 78.5 all-reduce.14
  765.1 115.3 reduce-scatter.5
  1016.0 68.5 all-reduce.16
  1087.2 78.5 all-reduce.18
  1169.8 115.3 reduce-scatter.7
where the time goes:
time: 1390 us
  blocking collectives  752 us (54%)
  waiting for transfers between devices  543 us (39%)
  other arithmetic  44.5 us (3%)
  matrix products  20 us (1%)
  between operations  15 us (1%)
    psum x3, blocking collectives, shards(): lax.psum(jnp.dot(member_own.T, basis_own, precision=highest), ('row', 'co...  239 us
    psum x3, blocking collectives, shards(): gram_matrix = lax.psum(gram_part, ('row', 'col'))  239 us
    psum x3, waiting for transfers between devices, shards(): rows_sum = lax.psum(part_rows, 'col')  233 us
    psum x3, waiting for transfers between devices, broadcast(): return lax.psum(jnp.where(mine, value, jnp.zeros_like(value)), axis)  198 us
    unnamed x1, blocking collectives  131 us
    all_gather x3, blocking collectives, shards(): lax.all_gather((inv_own[:, None] * basis_own).astype(jnp.bfloat16), 'row'...  126 us
    reduce_scatter x3, waiting for transfers between devices, shards(): lax.psum_scatter(part_cols, 'row', scatter_dimension=0, tiled=True)  111 us
  transfers between devices with their start and end apart: 9, of which 9 were waited for; matrix products, arithmetic and copies ran while one was open for 1% of the time, Pallas kernels for 0%

commit v1 on v0

--- a/solution.py
+++ b/solution.py
@@ -106,7 +106,7 @@
         part_rows, part_cols = apply_tiles(
             affinity_tiles, pick_rows, pick_cols, scaled_rows, scaled_cols, col_blocks
         )
-        rows_sum = lax.psum(part_rows, "col")
+        rows_sum = jnp.sum(lax.all_gather(part_rows, axis_name="col"), axis=0)
         part_cols = add_block(part_cols, is_owner * rows_sum, offset)
         product_own = lax.psum_scatter(part_cols, "row", scatter_dimension=0, tiled=True)
         applied_own = inv_own[:, None] * product_own + jnp.dot(

time: 1390 us -> 1310 us (0.942)
  waiting for transfers between devices: 543 us -> 468 us
    psum x3 -> x0, waiting for transfers between devices: 233 us -> none  [shards(): rows_sum = lax.psum(part_rows, 'col')]
    all_gather x0 -> x3, waiting for transfers between devices: none -> 165 us  [shards(): rows_sum = jnp.sum(lax.all_gather(part_rows, axis_name='col'), axis=0)]
  transfers between devices with their start and end apart: 9 -> 9, of which waited for: 9 -> 9; matrix products, arithmetic and copies ran while one was open for 1% -> 2% of each run, Pallas kernels for 0% -> 0%
where the time goes in v1:
time: 1310 us
  blocking collectives  748 us (57%)
  waiting for transfers between devices  468 us (36%)
  other arithmetic  46.9 us (4%)
  matrix products  19.9 us (2%)
  between operations  15 us (1%)
    psum x3, blocking collectives, shards(): gram_matrix = lax.psum(gram_part, ('row', 'col'))  239 us
    psum x3, blocking collectives, shards(): lax.psum(jnp.dot(member_own.T, basis_own, precision=highest), ('row', 'co...  236 us
    psum x3, waiting for transfers between devices, broadcast(): return lax.psum(jnp.where(mine, value, jnp.zeros_like(value)), axis)  198 us
    all_gather x3, waiting for transfers between devices, shards(): rows_sum = jnp.sum(lax.all_gather(part_rows, axis_name='col'), axis=0)  165 us
    unnamed x1, blocking collectives  131 us
    all_gather x3, blocking collectives, shards(): lax.all_gather((inv_own[:, None] * basis_own).astype(jnp.bfloat16), 'row'...  126 us
    reduce_scatter x3, waiting for transfers between devices, shards(): lax.psum_scatter(part_cols, 'row', scatter_dimension=0, tiled=True)  106 us
  transfers between devices with their start and end apart: 9, of which 9 were waited for; matrix products, arithmetic and copies ran while one was open for 2% of the time, Pallas kernels for 0%

profile of v1, /device:TPU:1, one launch (start us, length us, event | category | flops | bytes accessed | tf_op | source)
XLA Modules:
  0.0 1310.6 jit_solution(14737165555125877866)
XLA Ops:
  8.6 2.2 convert_reduce_fusion
  11.0 16.9 %psum.77 = f32[1024]{0:T(1024)S(1)} all-reduce(f32[1024]{0:T(1024)S(1)} %bitcast.169), channel_id=1, replica_groups=mesh['row'=32,'col'=8] {'col'}, use_global_device_ids=true, to_apply=%region_2.3 | all-reduce | flops 1024 | bytes 8192 | tf_op jit(solution)/shard_map/psum | solution.py:88
  28.1 130.8 %all-reduce = f32[4096]{0:T(1024)S(1)} all-reduce(f32[4096]{0:T(1024)S(1)} %add_dynamic-update-slice_fusion.3), channel_id=2, replica_groups=mesh['row'=32,'col'=8] {'row'}, use_global_device_ids=true, to_apply=%region_3.4.clone | all-reduce | flops 4096 | bytes 32768
  160.8 43.6 %all_gather.18 = bf16[4096,64]{0,1:T(8,128)(2,1)S(1)} all-gather(bf16[128,64]{0,1:T(8,128)(2,1)S(1)} %fusion.39), channel_id=1, replica_groups=mesh['row'=32,'col'=8] {'row'}, dimensions={0}, use_global_device_ids=true | all-gather | bytes 540672 | tf_op jit(solution)/shard_map/all_gather | solution.py:100
  206.5 0.9 fusion.8
  207.4 1.0 all_gather_reshape.9
  208.4 67.1 %all-reduce.6.cloned.1.call-done = bf16[2,512,64]{1,0,2:T(2,128)(2,1)} async-done(((bf16[2,512,64]{1,0,2:T(2,128)(2,1)}), bf16[2,512,64]{1,0,2:T(2,128)(2,1)}) %all-reduce.6.cloned.1.call-update) | async-done | bytes 131088 | tf_op jit(solution)/shard_map/psum | solution.py:13
  275.5 1.2 convolution_convert_fusion.5
  277.3 1.0 fusion.10
  278.9 54.9 %all-gather.4.cloned.1.call-done = f32[8,1024,64]{1,2,0:T(8,128)} async-done(((f32[1,1024,64]{1,2,0:T(8,128)}), f32[8,1024,64]{1,2,0:T(8,128)}) %all-gather.4.cloned.1.call-update) | async-done | bytes 2097168 | tf_op jit(solution)/shard_map/all_gather | solution.py:109
  333.8 1.8 reduce_sum.56
  335.6 1.0 copy-done.2
  337.2 78.7 %all-reduce.1 = (f32[32,64]{1,0:T(8,128)S(1)}, f32[]{:T(128)}) all-reduce(f32[32,64]{1,0:T(8,128)S(1)} %fusion.22, f32[]{:T(128)} %get-tuple-element.11), channel_id=1, replica_groups=mesh['row'=32,'col'=8] {'row','col'}, use_global_device_ids=true, to_apply=%region_10.11 | all-reduce | flops 2049 | bytes 16392 | tf_op jit(solution)/shard_map/psum | solution.py:98
  416.6 34.5 %reduce-scatter.4.cloned.1.call-done = f32[128,64]{0,1:T(8,128)} async-done(((f32[4096,64]{0,1:T(8,128)}), f32[128,64]{0,1:T(8,128)}) %reduce-scatter.4.cloned.1.call-update) | async-done | bytes 32784 | tf_op jit(solution)/shard_map/reduce_scatter | solution.py:111
  451.1 1.1 convolution_add_fusion.2
  452.4 79.7 %psum.81 = f32[64,64]{0,1:T(8,128)S(1)} all-reduce(f32[64,64]{0,1:T(8,128)S(1)} %fusion.75), channel_id=1, replica_groups=mesh['row'=32,'col'=8] {'row','col'}, use_global_device_ids=true, to_apply=%region_11.12 | all-reduce | flops 4096 | bytes 32768 | tf_op jit(solution)/shard_map/psum | solution.py:116
  532.2 5.8 cholesky.59
  539.4 4.9 custom-call.7
  544.5 41.2 %all_gather.20 = bf16[4096,64]{0,1:T(8,128)(2,1)S(1)} all-gather(bf16[128,64]{0,1:T(8,128)(2,1)S(1)} %fusion.44), channel_id=1, replica_groups=mesh['row'=32,'col'=8] {'row'}, dimensions={0}, use_global_device_ids=true | all-gather | bytes 540672 | tf_op jit(solution)/shard_map/all_gather | solution.py:100
  587.9 0.9 fusion.4
  588.8 1.0 all_gather_reshape.10
  589.9 65.3 %all-reduce.8.cloned.1.call-done = bf16[2,512,64]{1,0,2:T(2,128)(2,1)} async-done(((bf16[2,512,64]{1,0,2:T(2,128)(2,1)}), bf16[2,512,64]{1,0,2:T(2,128)(2,1)}) %all-reduce.8.cloned.1.call-update) | async-done | bytes 131088 | tf_op jit(solution)/shard_map/psum | solution.py:13
  655.1 1.2 convolution_convert_fusion.4
  656.8 1.0 fusion.6
  658.4 54.8 %all-gather.6.cloned.1.call-done = f32[8,1024,64]{1,2,0:T(8,128)} async-done(((f32[1,1024,64]{1,2,0:T(8,128)}), f32[8,1024,64]{1,2,0:T(8,128)}) %all-gather.6.cloned.1.call-update) | async-done | bytes 2097168 | tf_op jit(solution)/shard_map/all_gather | solution.py:109
  713.2 1.8 reduce_sum.58
  715.1 1.0 copy-done.3
  716.4 78.6 %psum.83 = f32[32,64]{1,0:T(8,128)S(1)} all-reduce(f32[32,64]{1,0:T(8,128)S(1)} %fusion.20), channel_id=1, replica_groups=mesh['row'=32,'col'=8] {'row','col'}, use_global_device_ids=true, to_apply=%region_17.20 | all-reduce | flops 2048 | bytes 16384 | tf_op jit(solution)/shard_map/psum | solution.py:98
  794.9 35.5 %reduce-scatter.6.cloned.1.call-done = f32[128,64]{0,1:T(8,128)} async-done(((f32[4096,64]{0,1:T(8,128)}), f32[128,64]{0,1:T(8,128)}) %reduce-scatter.6.cloned.1.call-update) | async-done | bytes 32784 | tf_op jit(solution)/shard_map/reduce_scatter | solution.py:111
  830.5 1.1 convolution_add_fusion.1
  831.7 79.7 %psum.84 = f32[64,64]{0,1:T(8,128)S(1)} all-reduce(f32[64,64]{0,1:T(8,128)S(1)} %fusion.76), channel_id=1, replica_groups=mesh['row'=32,'col'=8] {'row','col'}, use_global_device_ids=true, to_apply=%region_18.21 | all-reduce | flops 4096 | bytes 32768 | tf_op jit(solution)/shard_map/psum | solution.py:116
  911.5 5.8 cholesky.70
  918.7 4.9 custom-call.8
  923.9 41.2 %all_gather.22 = bf16[4096,64]{0,1:T(8,128)(2,1)S(1)} all-gather(bf16[128,64]{0,1:T(8,128)(2,1)S(1)} %fusion.45), channel_id=1, replica_groups=mesh['row'=32,'col'=8] {'row'}, dimensions={0}, use_global_device_ids=true | all-gather | bytes 540672 | tf_op jit(solution)/shard_map/all_gather | solution.py:100
  967.1 0.9 fusion
  968.0 1.0 all_gather_reshape.11
  969.3 65.2 %all-reduce.10.cloned.1.call-done = bf16[2,512,64]{1,0,2:T(2,128)(2,1)} async-done(((bf16[2,512,64]{1,0,2:T(2,128)(2,1)}), bf16[2,512,64]{1,0,2:T(2,128)(2,1)}) %all-reduce.10.cloned.1.call-update) | async-done | bytes 131088 | tf_op jit(solution)/shard_map/psum | solution.py:13
  1034.5 1.2 convolution_convert_fusion.3
  1036.2 1.0 fusion.2
  1037.8 54.9 %all-gather.8.cloned.1.call-done = f32[8,1024,64]{1,2,0:T(8,128)} async-done(((f32[1,1024,64]{1,2,0:T(8,128)}), f32[8,1024,64]{1,2,0:T(8,128)}) %all-gather.8.cloned.1.call-update) | async-done | bytes 2097168 | tf_op jit(solution)/shard_map/all_gather | solution.py:109
  1092.7 1.8 reduce_sum.59
  1094.6 1.0 copy-done.1
  1095.8 78.4 %psum.86 = f32[32,64]{1,0:T(8,128)S(1)} all-reduce(f32[32,64]{1,0:T(8,128)S(1)} %fusion.18), channel_id=1, replica_groups=mesh['row'=32,'col'=8] {'row','col'}, use_global_device_ids=true, to_apply=%region_22.25 | all-reduce | flops 2048 | bytes 16384 | tf_op jit(solution)/shard_map/psum | solution.py:98
  1174.2 35.8 %reduce-scatter.8.cloned.1.call-done = f32[128,64]{0,1:T(8,128)} async-done(((f32[4096,64]{0,1:T(8,128)}), f32[128,64]{0,1:T(8,128)}) %reduce-scatter.8.cloned.1.call-update) | async-done | bytes 32784 | tf_op jit(solution)/shard_map/reduce_scatter | solution.py:111
  1210.1 1.1 convolution_add_fusion
  1211.3 79.7 %psum.87 = f32[64,64]{0,1:T(8,128)S(1)} all-reduce(f32[64,64]{0,1:T(8,128)S(1)} %fusion.77), channel_id=1, replica_groups=mesh['row'=32,'col'=8] {'row','col'}, use_global_device_ids=true, to_apply=%region_23.26 | all-reduce | flops 4096 | bytes 32768 | tf_op jit(solution)/shard_map/psum | solution.py:116
  1291.1 5.8 cholesky.81
  1298.3 4.9 custom-call.9
  (100 shorter events, 21.0 us)
Async XLA Ops:
  6.5 152.4 %copy-start.6 = (u32[256]{0:T(256)S(1)}, u32[256]{0:T(256)}, u32[]{:S(2)}) copy-start(u32[256]{0:T(256)} %constant.105) | copy-start | bytes 3076
  6.5 154.3 %copy-start.4 = (f32[1,128,64]{1,2,0:T(8,128)S(1)}, f32[1,128,64]{1,2,0:T(8,128)}, u32[]{:S(2)}) copy-start(f32[1,128,64]{1,2,0:T(8,128)} %param.12) | copy-start | bytes 98308
  6.5 269.0 %all-reduce.6.cloned.1.call-start = ((), (), s32[]{:S(2)}) async-start(), calls=%async_computation.3 | async-start | bytes 262144 | tf_op jit(solution)/shard_map/psum | solution.py:13
  10.8 194.9 %copy-start = (bf16[4,512,512]{2,1,0:T(8,128)(2,1)S(1)}, bf16[4,512,512]{2,1,0:T(8,128)(2,1)}, u32[]{:S(2)}) copy-start(bf16[4,512,512]{2,1,0:T(8,128)(2,1)} %param.8) | copy-start | bytes 6291460
  205.2 128.6 %all-gather.4.cloned.1.call-start = ((), (), s32[]{:S(2)}) async-start(), calls=%async_computation.4 | async-start | bytes 2359296 | tf_op jit(solution)/shard_map/all_gather | solution.py:109
  208.4 242.7 %reduce-scatter.4.cloned.1.call-start = ((), (), s32[]{:S(2)}) async-start(), calls=%async_computation.5 | async-start | bytes 1081344 | tf_op jit(solution)/shard_map/reduce_scatter | solution.py:111
  278.9 57.8 %copy-start.5 = (s32[32]{0:T(128)S(1)}, s32[32]{0:T(128)}, u32[]{:S(2)}) copy-start(s32[32]{0:T(128)} %param.11) | copy-start | bytes 388
  335.6 1.0 copy-start.2
  336.6 318.5 %all-reduce.8.cloned.1.call-start = ((), (), s32[]{:S(2)}) async-start(), calls=%async_computation.6 | async-start | bytes 262144 | tf_op jit(solution)/shard_map/psum | solution.py:13
  586.5 126.7 %all-gather.6.cloned.1.call-start = ((), (), s32[]{:S(2)}) async-start(), calls=%async_computation.7 | async-start | bytes 2359296 | tf_op jit(solution)/shard_map/all_gather | solution.py:109
  589.8 240.6 %reduce-scatter.6.cloned.1.call-start = ((), (), s32[]{:S(2)}) async-start(), calls=%async_computation.8 | async-start | bytes 1081344 | tf_op jit(solution)/shard_map/reduce_scatter | solution.py:111
  715.1 1.0 copy-start.3
  716.1 318.4 %all-reduce.10.cloned.1.call-start = ((), (), s32[]{:S(2)}) async-start(), calls=%async_computation.9 | async-start | bytes 262144 | tf_op jit(solution)/shard_map/psum | solution.py:13
  965.8 126.9 %all-gather.8.cloned.1.call-start = ((), (), s32[]{:S(2)}) async-start(), calls=%async_computation.10 | async-start | bytes 2359296 | tf_op jit(solution)/shard_map/all_gather | solution.py:109
  969.0 241.1 %reduce-scatter.8.cloned.1.call-start = ((), (), s32[]{:S(2)}) async-start(), calls=%async_computation.11 | async-start | bytes 1081344 | tf_op jit(solution)/shard_map/reduce_scatter | solution.py:111
  1094.5 1.0 copy-start.1
Sparse Core Ops, SparseCore 0:
  205.3 70.1 all-reduce.5
  277.3 56.4 all-gather.3
  337.9 113.1 reduce-scatter.3
  586.6 68.4 all-reduce.7
  656.8 56.4 all-gather.5
  717.2 113.2 reduce-scatter.5
  966.0 68.4 all-reduce.9
  1036.3 56.4 all-gather.7
  1096.8 113.1 reduce-scatter.7
